TPU v7x, 512 devices: a whole 4x8x8 slice. The times are simulated.
512 devices in a mesh: wide: 32 (over z, x), narrow: 16 (over y, core).
Axes of the slice: x: 4, y: 8, z: 8, core: 2. Of those that a mesh axis runs over, the one named last changes fastest.
Arguments:
- tokens: bfloat16 [1024, 16384], P('wide', 'narrow'), may hold values from -200 to 200
- norm_gain: float32 [16384], P('narrow'), may hold values from 0.25 to 1.75
- gate_weight: bfloat16 [26624, 16384], P('wide', 'narrow'), may hold values from -0.046875 to 0.046875
- up_weight: bfloat16 [26624, 16384], P('wide', 'narrow'), may hold values from -0.046875 to 0.046875
- down_weight: bfloat16 [26624, 16384], P('wide', 'narrow'), may hold values from -0.0390625 to 0.0390625
Outputs:
- ffn_out: bfloat16 [1024, 16384], P('wide', 'narrow')
All inputs are finite; a program needn't handle non-finite values.
Results may differ from a plain program's by a relative error of at most 0.03.
Values may be sent and summed in bfloat16 or wider, within the bound.
No kernel may reach another device: no remote copies, remote signals or barrier semaphores. Data moves between devices by JAX's collectives and lax.ppermute only.
A program may use at most 64 MiB of HBM per device.

v0:
```python
import jax
import jax.numpy as jnp
from jax import lax
from jax.sharding import PartitionSpec as P

D = 16384
EPS = 1e-05


def project_pair(rows, gate_weight, up_weight):
    dims = (((1,), (1,)), ((), ()))
    gate = lax.dot_general(rows, gate_weight, dims, preferred_element_type=jnp.float32)
    upward = lax.dot_general(rows, up_weight, dims, preferred_element_type=jnp.float32)
    return jnp.concatenate([gate, upward], axis=1)


def activate(sums, width):
    return (jax.nn.silu(sums[:, :width]) * sums[:, width:]).astype(jnp.bfloat16)


def local(tokens, norm_gain, gate_weight, up_weight, down_weight):
    width = gate_weight.shape[0]
    whole = lax.all_gather(tokens, "wide", axis=0, tiled=True)
    values = whole.astype(jnp.float32)
    squares = lax.psum(jnp.sum(values * values, axis=1), "narrow")
    normed = (values * lax.rsqrt(squares[:, None] / D + EPS) * norm_gain).astype(jnp.bfloat16)
    sums = lax.psum(
        project_pair(normed, gate_weight, up_weight).astype(jnp.bfloat16), "narrow"
    ).astype(jnp.float32)
    hidden = activate(sums, width)
    return lax.psum_scatter(
        jnp.dot(hidden, down_weight, preferred_element_type=jnp.float32).astype(jnp.bfloat16),
        "wide",
        scatter_dimension=0,
        tiled=True,
    )


def solution(mesh):
    in_specs = (
        P("wide", "narrow"),
        P("narrow"),
        P("wide", "narrow"),
        P("wide", "narrow"),
        P("wide", "narrow"),
    )
    out_specs = P("wide", "narrow")
    return jax.shard_map(local, mesh=mesh, in_specs=in_specs, out_specs=out_specs, check_vma=False)
```

profile of v0, /device:TPU:8, one launch (start us, length us, event | category | flops | bytes accessed | tf_op | source)
XLA Modules:
  0.0 490.7 jit_solution(1981325503855157326)
XLA Ops:
  6.5 0.0 copy-start
  6.5 0.0 all-gather.2.cloned.1.call-start
  6.5 0.7 all-gather.2.cloned.1.call-update
  7.3 0.0 all-reduce.2.cloned.1.call-start
  7.3 91.8 %all-gather.2.cloned.1.call-done = bf16[1024,1024]{1,0:T(8,128)(2,1)} async-done(((bf16[32,1024]{1,0:T(8,128)(2,1)}), bf16[1024,1024]{1,0:T(8,128)(2,1)}) %all-gather.2.cloned.1.call-update) | async-done | bytes 2097168 | tf_op jit(solution)/shard_map/all_gather | solution.py:23
  99.1 2.1 fusion
  101.2 20.6 %psum.14 = f32[1024]{0:T(1024)S(1)} all-reduce(f32[1024]{0:T(1024)S(1)} %fusion), channel_id=1, replica_groups=mesh['wide'=32,'narrow'=16] {'narrow'}, use_global_device_ids=true, to_apply=%region_1.0 | all-reduce | flops 1024 | bytes 8192 | tf_op jit(solution)/shard_map/psum | solution.py:25
  121.8 0.0 copy-start.1
  121.8 0.0 copy-start.2
  121.8 0.0 copy-start.3
  121.9 4.3 convolution_convert_fusion.1
  126.2 0.0 copy-done.1
  126.2 0.0 copy-done.2
  126.2 0.0 copy-done.3
  126.2 2.1 convolution_convert_fusion.2
  128.3 2.1 pad_maximum_fusion
  130.4 0.0 all-reduce.2.cloned.1.call-update
  130.4 0.0 reduce-scatter.2.cloned.1.call-start
  130.5 121.9 %all-reduce.2.cloned.1.call-done = bf16[1024,1664]{0,1:T(8,128)(2,1)} async-done(((bf16[1024,1664]{0,1:T(8,128)(2,1)}), bf16[1024,1664]{0,1:T(8,128)(2,1)}) %all-reduce.2.cloned.1.call-update) | async-done | bytes 3407888 | tf_op jit(solution)/shard_map/psum | solution.py:27
  252.4 2.8 convert_element_type.18
  255.2 0.0 copy-done
  255.2 3.9 convolution_convert_fusion
  259.0 0.0 reduce-scatter.2.cloned.1.call-update
  259.1 225.1 %reduce-scatter.2.cloned.1.call-done = bf16[32,1024]{1,0:T(8,128)(2,1)} async-done(((bf16[1024,1024]{1,0:T(8,128)(2,1)}), bf16[32,1024]{1,0:T(8,128)(2,1)}) %reduce-scatter.2.cloned.1.call-update) | async-done | bytes 65552 | tf_op jit(solution)/shard_map/reduce_scatter | solution.py:31
  (1 shorter events, 0.0 us)
Async XLA Ops:
  6.5 248.6 %copy-start = (bf16[832,1024]{1,0:T(8,128)(2,1)S(1)}, bf16[832,1024]{1,0:T(8,128)(2,1)}, u32[]{:S(2)}) copy-start(bf16[832,1024]{1,0:T(8,128)(2,1)} %param.9) | copy-start | bytes 5111812
  6.5 92.6 %all-gather.2.cloned.1.call-start = ((), (), s32[]{:S(2)}) async-start(), calls=%async_computation.1 | async-start | bytes 2162688 | tf_op jit(solution)/shard_map/all_gather | solution.py:23
  7.3 245.1 %all-reduce.2.cloned.1.call-start = ((), (), s32[]{:S(2)}) async-start(), calls=%async_computation.2 | async-start | bytes 6815744 | tf_op jit(solution)/shard_map/psum | solution.py:27
  121.8 4.3 copy-start.1
  121.8 4.3 copy-start.2
  121.8 4.3 copy-start.3
  130.4 353.8 %reduce-scatter.2.cloned.1.call-start = ((), (), s32[]{:S(2)}) async-start(), calls=%async_computation.3 | async-start | bytes 2162688 | tf_op jit(solution)/shard_map/reduce_scatter | solution.py:31
Sparse Core Ops, SparseCore 0:
  10.5 88.5 all-gather.1
  130.6 121.7 all-reduce.1
  259.2 224.9 reduce-scatter.1
where the time goes:
time: 491 us
  waiting for transfers between devices  440 us (90%)
  blocking collectives  20.6 us (4%)
  between operations  13.2 us (3%)
  matrix products  10.3 us (2%)
  other arithmetic  6.94 us (1%)
    reduce_scatter x1, waiting for transfers between devices, local(): lax.psum_scatter(jnp.dot(hidden, down_weight, preferred_element_type=jnp....  225 us
    psum x1, waiting for transfers between devices, local(): lax.psum(project_pair(normed, gate_weight, up_weight).astype(jnp.bfloat16...  122 us
    all_gather x1, waiting for transfers between devices, local(): whole = lax.all_gather(tokens, 'wide', axis=0, tiled=True)  91.8 us
    psum x1, blocking collectives, local(): squares = lax.psum(jnp.sum(values * values, axis=1), 'narrow')  20.6 us
  transfers between devices with their start and end apart: 3, of which 3 were waited for; matrix products, arithmetic and copies ran while one was open for 0% of the time, Pallas kernels for 0%

commit v1 on v0

--- a/solution.py
+++ b/solution.py
@@ -20,7 +20,11 @@
 
 def local(tokens, norm_gain, gate_weight, up_weight, down_weight):
     width = gate_weight.shape[0]
-    whole = lax.all_gather(tokens, "wide", axis=0, tiled=True)
+    size = lax.axis_size("wide")
+    repeats = [size if d == 0 else 1 for d in range(tokens.ndim)]
+    whole = lax.all_to_all(
+        jnp.tile(tokens, repeats), "wide", split_axis=0, concat_axis=0, tiled=True
+    )
     values = whole.astype(jnp.float32)
     squares = lax.psum(jnp.sum(values * values, axis=1), "narrow")
     normed = (values * lax.rsqrt(squares[:, None] / D + EPS) * norm_gain).astype(jnp.bfloat16)

time: 491 us -> 463 us (0.943)
  waiting for transfers between devices: 440 us -> 346 us
  blocking collectives: 20.6 us -> 84.8 us
    all_gather x1 -> x0, waiting for transfers between devices: 91.8 us -> none  [local(): whole = lax.all_gather(tokens, 'wide', axis=0, tiled=True)]
    all_to_all x0 -> x1, blocking collectives: none -> 63.5 us  [local(): lax.all_to_all(jnp.tile(tokens, repeats), 'wide', split_axis=0, concat_ax...]
  transfers between devices with their start and end apart: 3 -> 2, of which waited for: 3 -> 2; matrix products, arithmetic and copies ran while one was open for 0% -> 0% of each run, Pallas kernels for 0% -> 0%
where the time goes in v1:
time: 463 us
  waiting for transfers between devices  346 us (75%)
  blocking collectives  84.8 us (18%)
  between operations  13.5 us (3%)
  matrix products  7.9 us (2%)
  other arithmetic  7.6 us (2%)
    reduce_scatter x1, waiting for transfers between devices, local(): lax.psum_scatter(jnp.dot(hidden, down_weight, preferred_element_type=jnp....  225 us
    psum x1, waiting for transfers between devices, local(): lax.psum(project_pair(normed, gate_weight, up_weight).astype(jnp.bfloat16...  121 us
    all_to_all x1, blocking collectives, local(): lax.all_to_all(jnp.tile(tokens, repeats), 'wide', split_axis=0, concat_ax...  63.5 us
    psum x1, blocking collectives, local(): squares = lax.psum(jnp.sum(values * values, axis=1), 'narrow')  21.2 us
  transfers between devices with their start and end apart: 2, of which 2 were waited for; matrix products, arithmetic and copies ran while one was open for 0% of the time, Pallas kernels for 0%

profile of v1, /device:TPU:8, one launch (start us, length us, event | category | flops | bytes accessed | tf_op | source)
XLA Modules:
  0.0 462.8 jit_solution(7485414060389519266)
XLA Ops:
  6.5 0.0 copy-start
  6.5 0.0 all-reduce.2.cloned.1.call-start
  6.5 1.2 tile.2
  7.8 63.5 %all_to_all.6 = bf16[32,32,1024]{2,1,0:T(8,128)(2,1)S(1)} all-to-all(bf16[32,32,1024]{2,1,0:T(8,128)(2,1)S(1)} %tile.2), channel_id=1, replica_groups=mesh['wide'=32,'narrow'=16] {'wide'}, dimensions={0} | all-to-all | bytes 4194304 | tf_op jit(solution)/shard_map/all_to_all | solution.py:25
  71.3 0.0 copy-start.1
  71.3 1.3 copy-done.1
  72.6 0.0 copy-start.2
  72.6 0.5 multiply_reduce_fusion
  73.1 0.1 reduce_sum.12
  73.2 21.2 %psum.14 = f32[1024]{0:T(1024)S(1)} all-reduce(f32[1024]{0:T(1024)S(1)} %reduce_sum.12), channel_id=1, replica_groups=mesh['wide'=32,'narrow'=16] {'narrow'}, use_global_device_ids=true, to_apply=%region_1.0 | all-reduce | flops 1024 | bytes 8192 | tf_op jit(solution)/shard_map/psum | solution.py:29
  94.4 0.0 copy-done.2
  94.4 0.0 copy-start.3
  94.5 2.3 fusion.1
  96.7 0.0 copy-done.3
  96.7 0.0 copy-start.4
  96.7 2.0 convolution_convert_fusion.1
  98.8 0.0 copy-done.4
  98.8 2.0 convolution_convert_fusion.2
  100.8 2.1 pad_maximum_fusion
  102.9 0.0 all-reduce.2.cloned.1.call-update
  102.9 0.0 reduce-scatter.2.cloned.1.call-start
  103.0 121.4 %all-reduce.2.cloned.1.call-done = bf16[1024,1664]{0,1:T(8,128)(2,1)} async-done(((bf16[1024,1664]{0,1:T(8,128)(2,1)}), bf16[1024,1664]{0,1:T(8,128)(2,1)}) %all-reduce.2.cloned.1.call-update) | async-done | bytes 3407888 | tf_op jit(solution)/shard_map/psum | solution.py:31
  224.3 2.8 convert_element_type.26
  227.1 0.0 copy-done
  227.1 3.9 convolution_convert_fusion
  231.0 0.0 reduce-scatter.2.cloned.1.call-update
  231.0 224.9 %reduce-scatter.2.cloned.1.call-done = bf16[32,1024]{1,0:T(8,128)(2,1)} async-done(((bf16[1024,1024]{1,0:T(8,128)(2,1)}), bf16[32,1024]{1,0:T(8,128)(2,1)}) %reduce-scatter.2.cloned.1.call-update) | async-done | bytes 65552 | tf_op jit(solution)/shard_map/reduce_scatter | solution.py:35
  (1 shorter events, 0.0 us)
Async XLA Ops:
  6.5 220.6 %copy-start = (bf16[832,1024]{1,0:T(8,128)(2,1)S(1)}, bf16[832,1024]{1,0:T(8,128)(2,1)}, u32[]{:S(2)}) copy-start(bf16[832,1024]{1,0:T(8,128)(2,1)} %param.9) | copy-start | bytes 5111812
  6.5 217.8 %all-reduce.2.cloned.1.call-start = ((), (), s32[]{:S(2)}) async-start(), calls=%async_computation.2 | async-start | bytes 6815744 | tf_op jit(solution)/shard_map/psum | solution.py:31
  71.3 1.4 copy-start.1
  72.6 21.8 %copy-start.2 = (f32[1024]{0:T(1024)S(1)}, f32[1024]{0:T(1024)}, u32[]{:S(2)}) copy-start(f32[1024]{0:T(1024)} %param.6) | copy-start | bytes 12292
  94.4 2.3 copy-start.3
  96.7 2.0 copy-start.4
  102.9 353.0 %reduce-scatter.2.cloned.1.call-start = ((), (), s32[]{:S(2)}) async-start(), calls=%async_computation.3 | async-start | bytes 2162688 | tf_op jit(solution)/shard_map/reduce_scatter | solution.py:35
Sparse Core Ops, SparseCore 0:
  103.0 121.2 all-reduce.1
  231.1 224.7 reduce-scatter.1
